TPU v7x, 128 devices: a whole 4x4x4 slice. The times are simulated.
128 devices in a mesh: dp: 16 (over x, y_hi, core), tensor: 8 (over y_lo, z).
Axes of the slice: x: 4, y: 4 (y_hi: 2, y_lo: 2; y = y_hi * 2 + y_lo), z: 4, core: 2. Of those that a mesh axis runs over, the one named last changes fastest.
Arguments:
- hidden_state_input: bfloat16 [16384, 3584], P(('dp', 'tensor')), may hold values from -500 to 500
- token_embedding_input: bfloat16 [16384, 3584], P(('dp', 'tensor')), may hold values from -500 to 500
- input_norm_gain: float32 [7168], replicated, may hold values from 0.1 to 1.9
- query_projection_weight: bfloat16 [7168, 3584], P('dp', 'tensor'), may hold values from -0.0625 to 0.0625
- key_projection_weight: bfloat16 [7168, 3584], P('dp', 'tensor'), may hold values from -0.0625 to 0.0625
- value_projection_weight: bfloat16 [7168, 3584], P('dp', 'tensor'), may hold values from -0.0625 to 0.0625
- adapter_down_maps: bfloat16 [7168, 384], replicated, may hold values from -1 to 1
- adapter_up_maps: bfloat16 [3, 128, 3584], P(None, None, 'tensor'), may hold values from -2 to 2
- output_projection_weight: bfloat16 [3584, 3584], P('tensor'), may hold values from -0.09375 to 0.09375
- segment: int32 [16384], P('dp'), may hold values from 0 to 3, as said below
- live_token_length: int32 [16], P('dp'), may hold values from 512 to 1024, as said below
- request_cache_row: int32 [64], P('dp'), may hold values from 0 to 63, as said below
Outputs:
- block_out: bfloat16 [16384, 3584], P(('dp', 'tensor'))
- kv_cache: bfloat16 [64, 256, 2, 3584], P(None, 'dp', None, 'tensor')
Inputs may be any that keep to these rules, and one draw needn't show every extreme that they name: `segment`: within a stream, the live slots carry request numbers that never fall, every request 0 to 3 appears, each on (257) // 2 to 256 slots, some request in every draw on exactly 256; slots at or past live_token_length hold 3. `live_token_length`: each stream's live tokens; some stream is full in every draw. `request_cache_row`: A permutation of the 64 cache rows.
All inputs are finite; a program needn't handle non-finite values.
Results may differ from a plain program's by a relative error of at most 0.015.
The roundings to bfloat16 on the way count: a program that leaves them out, or rounds other values in their place, can miss the bound.
Values may be sent and summed in bfloat16 or wider, within the bound.
No kernel may reach another device: no remote copies, remote signals or barrier semaphores. Data moves between devices by JAX's collectives and lax.ppermute only.
A program may use at most 128 MiB of HBM per device.

v0:
```python
import math
import jax
import jax.numpy as jnp
from jax import lax
from jax.sharding import PartitionSpec as P

HD = 224
epsilon = 1e-05
negative = -1e30


def normalize(hidden_state_input, token_embedding_input, input_norm_gain):
    combined = jnp.concatenate([hidden_state_input, token_embedding_input], 1).astype(jnp.float32)
    factor = lax.rsqrt(jnp.mean(combined * combined, axis=1, keepdims=True) + epsilon)
    return (combined * factor * input_norm_gain).astype(jnp.bfloat16)


def attend_block(query, keys, values, segment, position, live, first, count, key_end):
    heads = query.shape[1] // HD
    block_query = query[first : first + count].reshape(count, heads, HD)
    block_keys = keys.reshape(key_end, heads, HD)
    block_values = values.reshape(key_end, heads, HD)
    scores = jnp.einsum(
        "qhd,khd->hqk", block_query, block_keys, preferred_element_type=jnp.float32
    ) / math.sqrt(HD)
    query_at = position[first : first + count]
    allowed = (
        (segment[first : first + count, None] == segment[None, :key_end])
        & (position[None, :] <= query_at[:, None])
        & (position[None, :] < live)
    )
    scores = jnp.where(allowed[None], scores, negative)
    top = jnp.max(scores, axis=-1, keepdims=True)
    expo = jnp.exp(scores - top)
    weights = (expo / jnp.sum(expo, axis=-1, keepdims=True)).astype(jnp.bfloat16)
    mixed = jnp.einsum("hqk,khd->qhd", weights, block_values, preferred_element_type=jnp.float32)
    mixed = jnp.where((query_at < live)[:, None, None], mixed, 0.0)
    return mixed.astype(jnp.bfloat16).reshape(count, heads * HD)


def body(
    hidden_state_input,
    token_embedding_input,
    input_norm_gain,
    query_projection_weight,
    key_projection_weight,
    value_projection_weight,
    adapter_down_maps,
    adapter_up_maps,
    output_projection_weight,
    segment,
    live_token_length,
    request_cache_row,
):
    adapter_rank_width = adapter_up_maps.shape[1]
    head_cols = query_projection_weight.shape[1]
    normalized_hidden = normalize(hidden_state_input, token_embedding_input, input_norm_gain)
    adapter_update = jnp.dot(
        normalized_hidden, adapter_down_maps, preferred_element_type=jnp.float32
    ).astype(jnp.bfloat16)
    stream_in, stream_low = (
        lax.all_gather(normalized_hidden, "tensor", axis=0, tiled=True),
        lax.all_gather(adapter_update, "tensor", axis=0, tiled=True),
    )
    pieces = (
        lax.all_gather(query_projection_weight, "dp", axis=0, tiled=True),
        lax.all_gather(key_projection_weight, "dp", axis=0, tiled=True),
        lax.all_gather(value_projection_weight, "dp", axis=0, tiled=True),
    )
    folded = tuple(
        (jnp.dot(stream_in, piece, preferred_element_type=jnp.float32) for piece in pieces)
    )
    projected = []
    for adapter_selector in range(3):
        adapter = jnp.dot(
            stream_low[
                :,
                adapter_selector * adapter_rank_width : (adapter_selector + 1) * adapter_rank_width,
            ],
            adapter_up_maps[adapter_selector],
            preferred_element_type=jnp.float32,
        )
        projected.append((folded[adapter_selector] + adapter).astype(jnp.bfloat16))
    query, keys, values = projected
    stream = query.shape[0]
    position = jnp.arange(stream, dtype=jnp.int32)
    live = live_token_length[0]
    block = min(512, stream)
    attended_parts = []
    for block_index in range(stream // block):
        first = block_index * block
        attended_parts.append(
            attend_block(query, keys, values, segment, position, live, first, block, stream)
        )
    attended = jnp.concatenate(attended_parts, 0)
    block_out = lax.psum_scatter(
        jnp.dot(attended, output_projection_weight, preferred_element_type=jnp.float32).astype(
            jnp.bfloat16
        ),
        "tensor",
        scatter_dimension=0,
        tiled=True,
    )
    requests = request_cache_row.shape[0]
    longest = stream // requests
    groups = lax.axis_size("dp")
    piece_len = longest // groups
    numbers = jnp.arange(requests, dtype=jnp.int32)
    membership = ((segment[:, None] == numbers[None, :]) & (position < live)[:, None]).astype(
        jnp.int32
    )
    lengths = jnp.sum(membership, axis=0)
    starts = jnp.cumsum(lengths) - lengths
    offsets = (
        jnp.arange(groups, dtype=jnp.int32)[:, None] * piece_len
        + jnp.arange(piece_len, dtype=jnp.int32)[None, :]
    )
    source_rows = jnp.minimum(starts[None, :, None] + offsets[:, None, :], stream - 1)
    alive_mask = offsets[:, None, :] < lengths[None, :, None]
    stacked = jnp.stack([keys, values], 1).reshape(stream, 2 * head_cols)
    taken = jnp.take(stacked, source_rows.reshape(-1), axis=0)
    taken = jnp.where(alive_mask.reshape(-1)[:, None], taken, jnp.zeros((), jnp.bfloat16))
    taken = taken.reshape(groups, requests, piece_len * 2 * head_cols)
    row_send = jnp.broadcast_to(request_cache_row[None, :], (groups, requests))
    received, received_rows = (
        lax.all_to_all(taken, "dp", split_axis=0, concat_axis=0, tiled=True),
        lax.all_to_all(row_send, "dp", split_axis=0, concat_axis=0, tiled=True),
    )
    total_reqs = groups * requests
    placing = (
        received_rows.reshape(-1)[:, None] == jnp.arange(total_reqs, dtype=jnp.int32)[None, :]
    ).astype(jnp.bfloat16)
    flat_received = received.reshape(total_reqs, piece_len * 2 * head_cols)
    cache_rows = lax.dot_general(
        placing, flat_received, (((0,), (0,)), ((), ())), preferred_element_type=jnp.float32
    )
    kv_cache = cache_rows.astype(jnp.bfloat16).reshape(total_reqs, piece_len, 2, head_cols)
    return (block_out, kv_cache)


def solution(mesh):
    return jax.shard_map(
        body,
        mesh=mesh,
        in_specs=(
            P(("dp", "tensor"), None),
            P(("dp", "tensor"), None),
            P(),
            P("dp", "tensor"),
            P("dp", "tensor"),
            P("dp", "tensor"),
            P(),
            P(None, None, "tensor"),
            P("tensor", None),
            P("dp"),
            P("dp"),
            P("dp"),
        ),
        out_specs=(P(("dp", "tensor"), None), P(None, "dp", None, "tensor")),
        check_vma=False,
    )
```

profile of v0, /device:TPU:1, one launch (start us, length us, event | category | flops | bytes accessed | tf_op | source)
XLA Modules:
  0.0 503.1 jit_solution(3945014618020465741)
XLA Ops:
  8.0 2.1 fusion.2
  10.0 3.2 fusion.4
  15.4 4.3 convolution_convert_fusion.2
  19.7 28.2 %all_gather.17 = bf16[1024,384]{1,0:T(8,128)(2,1)S(1)} all-gather(bf16[128,384]{1,0:T(8,128)(2,1)S(1)} %convolution_convert_fusion.2), channel_id=1, replica_groups=mesh['dp'=16,'tensor'=8] {'tensor'}, dimensions={0}, use_global_device_ids=true | all-gather | bytes 884736 | tf_op jit(solution)/shard_map/all_gather | solution.py:63
  47.9 1.7 fusion.30
  53.0 2.1 fusion.14
  55.1 27.7 %all-gather.9.cloned.1.call-done = bf16[7168,448]{1,0:T(8,128)(2,1)} async-done(((bf16[448,448]{1,0:T(8,128)(2,1)}), bf16[7168,448]{1,0:T(8,128)(2,1)}) %all-gather.9.cloned.1.call-update) | async-done | bytes 6422544 | tf_op jit(solution)/shard_map/all_gather | solution.py:66
  82.9 150.3 %all-gather.5.cloned.1.call-done = bf16[1024,7168]{1,0:T(8,128)(2,1)} async-done(((bf16[128,7168]{1,0:T(8,128)(2,1)}), bf16[1024,7168]{1,0:T(8,128)(2,1)}) %all-gather.5.cloned.1.call-update) | async-done | bytes 14680080 | tf_op jit(solution)/shard_map/all_gather | solution.py:62
  233.2 13.3 %add_convert_fusion.1 = bf16[1024,448]{0,1:T(8,128)(2,1)} fusion(f32[1024,448]{0,1:T(8,128)} %fusion.28, bf16[1024,7168]{1,0:T(8,128)(2,1)} %all-gather.5.cloned.1.call-done, bf16[7168,448]{1,0:T(8,128)(2,1)} %all-gather.9.cloned.1.call-done), kind=kOutput, calls=%fused_computation.36 | convolution fusion | flops 6577586176 | bytes 23855104 | tf_op jit(solution)/shard_map/dot_general | solution.py:71
  246.4 2.2 fusion.49
  248.6 54.5 %all-gather.11.cloned.1.call-done = bf16[7168,448]{1,0:T(8,128)(2,1)} async-done(((bf16[448,448]{1,0:T(8,128)(2,1)}), bf16[7168,448]{1,0:T(8,128)(2,1)}) %all-gather.11.cloned.1.call-update) | async-done | bytes 6422544 | tf_op jit(solution)/shard_map/all_gather | solution.py:67
  303.1 13.3 %add_convert_fusion = bf16[1024,448]{0,1:T(8,128)(2,1)} fusion(f32[1024,448]{0,1:T(8,128)} %fusion.26, bf16[1024,7168]{1,0:T(8,128)(2,1)} %all-gather.5.cloned.1.call-done, bf16[7168,448]{1,0:T(8,128)(2,1)} %all-gather.11.cloned.1.call-done), kind=kOutput, calls=%fused_computation.35 | convolution fusion | flops 6577586176 | bytes 23855104 | tf_op jit(solution)/shard_map/dot_general | solution.py:71
  316.4 5.2 %fusion.51 = (f32[2,512]{1,0:T(2,128)S(1)}, f32[2,512,1024]{2,1,0:T(8,128)}) fusion(pred[512,1024]{1,0:T(8,128)(4,1)} %get-tuple-element.7, bf16[512,2,224]{0,2,1:T(8,128)(2,1)} %bitcast.61, bf16[1024,2,224]{0,2,1:T(8,128)(2,1)} %bitcast.54), kind=kOutput, calls=%fused_computation.85 | convolution fusion | flops 473957376 | bytes 6098944 | tf_op jit(solution)/shard_map/sub | solution.py:34
  321.6 5.3 %fusion.52 = (f32[2,512]{1,0:T(2,128)S(1)}, f32[2,512,1024]{2,1,0:T(8,128)}) fusion(pred[512,1024]{1,0:T(8,128)(4,1)} %get-tuple-element.6, bf16[512,2,224]{0,2,1:T(8,128)(2,1)} %bitcast.60, bf16[1024,2,224]{0,2,1:T(8,128)(2,1)} %bitcast.55), kind=kOutput, calls=%fused_computation.86 | convolution fusion | flops 473957376 | bytes 6098944 | tf_op jit(solution)/shard_map/sub | solution.py:34
  326.9 44.8 %all-gather.7.cloned.1.call-done = bf16[7168,448]{1,0:T(8,128)(2,1)} async-done(((bf16[448,448]{1,0:T(8,128)(2,1)}), bf16[7168,448]{1,0:T(8,128)(2,1)}) %all-gather.7.cloned.1.call-update) | async-done | bytes 6422544 | tf_op jit(solution)/shard_map/all_gather | solution.py:68
  371.7 13.3 %add_convert_fusion.2 = bf16[1024,448]{0,1:T(8,128)(2,1)} fusion(f32[1024,448]{0,1:T(8,128)} %fusion.30, bf16[1024,7168]{1,0:T(8,128)(2,1)} %all-gather.5.cloned.1.call-done, bf16[7168,448]{1,0:T(8,128)(2,1)} %all-gather.7.cloned.1.call-done), kind=kOutput, calls=%fused_computation.37 | convolution fusion | flops 6577586176 | bytes 23855104 | tf_op jit(solution)/shard_map/dot_general | solution.py:71
  385.0 3.5 fusion.20
  390.0 6.1 %convolution_convert_fusion.1 = bf16[1024,3584]{1,0:T(8,128)(2,1)} fusion(bf16[448,3584]{1,0:T(8,128)(2,1)S(1)} %copy-done, bf16[512,448]{0,1:T(8,128)(2,1)S(1)} %bitcast.64, bf16[512,448]{0,1:T(8,128)(2,1)S(1)} %bitcast.65), kind=kOutput, calls=%fused_computation.4 | convolution fusion | flops 3293839360 | bytes 11468800 | tf_op jit(solution)/shard_map/dot_general | solution.py:97
  397.3 3.6 all-to-all-start
  402.7 4.0 broadcast_in_dim.106
  407.9 3.9 broadcast_in_dim.108
  412.0 2.9 pad_maximum_fusion.1
  414.9 3.9 copy.17
  418.8 7.5 %gather_fusion = bf16[1024,896]{1,0:T(8,128)(2,1)} fusion(bf16[1024,896]{1,0:T(8,128)(2,1)} %copy.17, s32[1024]{0:T(1024)S(1)} %broadcast_clamp_fusion), kind=kCustom, calls=%fused_computation | custom fusion | bytes 3674112 | tf_op jit(solution)/shard_map/jit(_take)/gather | solution.py:121
  426.3 4.4 gather.7
  430.6 5.5 %select_select_fusion = bf16[16,4,14336]{2,1,0:T(4,128)(2,1)} fusion(pred[16,4,14336]{2,1,0:T(4,128)(4,1)} %broadcast_in_dim.106, pred[16,4,14336]{2,1,0:T(4,128)(4,1)} %broadcast_in_dim.108, bf16[16,4,14336]{2,1,0:T(4,128)(2,1)} %gather.7), kind=kLoop, calls=%fused_computation.34 | loop fusion | flops 1835008 | bytes 5505024 | tf_op jit(solution)/shard_map/jit(_where)/select_n | solution.py:122
  436.2 7.1 %all-to-all-start.1 = ((bf16[16,4,14336]{2,1,0:T(4,128)(2,1)}), bf16[16,4,14336]{2,1,0:T(4,128)(2,1)}, u32[]{:S(2)}, u32[]{:S(2)}) async-start(bf16[16,4,14336]{2,1,0:T(4,128)(2,1)} %select_select_fusion), calls=%async_computation.2 | async-start | bytes 3670016 | tf_op jit(solution)/shard_map/all_to_all | solution.py:126
  444.5 28.2 %all-to-all-done.1 = bf16[16,4,14336]{2,1,0:T(4,128)(2,1)} async-done(((bf16[16,4,14336]{2,1,0:T(4,128)(2,1)}), bf16[16,4,14336]{2,1,0:T(4,128)(2,1)}, u32[]{:S(2)}, u32[]{:S(2)}) %all-to-all-start.1) | async-done | bytes 1835040 | tf_op jit(solution)/shard_map/all_to_all | solution.py:126
  472.7 3.9 reshape.308
  476.6 3.6 convolution_convert_fusion
  480.1 6.8 %reshape.309 = bf16[64,16,2,448]{3,2,1,0:T(2,128)(2,1)} reshape(bf16[64,14336]{1,0:T(8,128)(2,1)} %convolution_convert_fusion) | data formatting | bytes 3670016 | tf_op jit(solution)/shard_map/reshape | solution.py:137
  486.9 9.7 %reduce-scatter.2.cloned.1.call-done = bf16[128,3584]{1,0:T(8,128)(2,1)} async-done(((bf16[1024,3584]{1,0:T(8,128)(2,1)}), bf16[128,3584]{1,0:T(8,128)(2,1)}) %reduce-scatter.2.cloned.1.call-update) | async-done | bytes 917520 | tf_op jit(solution)/shard_map/reduce_scatter | solution.py:96
  (53 shorter events, 12.5 us)
Async XLA Ops:
  7.2 382.8 %copy-start = (bf16[448,3584]{1,0:T(8,128)(2,1)S(1)}, bf16[448,3584]{1,0:T(8,128)(2,1)}, u32[]{:S(2)}) copy-start(bf16[448,3584]{1,0:T(8,128)(2,1)} %param.20) | copy-start | bytes 9633796
  7.2 75.7 %all-gather.9.cloned.1.call-start = ((), (), s32[]{:S(2)}) async-start(), calls=%async_computation.5 | async-start | bytes 7798784 | tf_op jit(solution)/shard_map/all_gather | solution.py:66
  7.9 225.2 %all-gather.5.cloned.1.call-start = ((), (), s32[]{:S(2)}) async-start(), calls=%async_computation.3 | async-start | bytes 16515072 | tf_op jit(solution)/shard_map/all_gather | solution.py:62
  10.0 5.3 %copy-start.3 = (s32[1024]{0:T(1024)S(1)}, s32[1024]{0:T(1024)}, u32[]{:S(2)}) copy-start(s32[1024]{0:T(1024)} %param.21) | copy-start | bytes 12292
  13.3 289.8 %all-gather.11.cloned.1.call-start = ((), (), s32[]{:S(2)}) async-start(), calls=%async_computation.6 | async-start | bytes 7798784 | tf_op jit(solution)/shard_map/all_gather | solution.py:67
  14.0 357.7 %all-gather.7.cloned.1.call-start = ((), (), s32[]{:S(2)}) async-start(), calls=%async_computation.4 | async-start | bytes 7798784 | tf_op jit(solution)/shard_map/all_gather | solution.py:68
  14.6 482.0 %reduce-scatter.2.cloned.1.call-start = ((), (), s32[]{:S(2)}) async-start(), calls=%async_computation.7 | async-start | bytes 8257536 | tf_op jit(solution)/shard_map/reduce_scatter | solution.py:96
  14.7 5.0 %copy-start.4 = (s32[1024]{0:T(1024)}, s32[1024]{0:T(1024)S(1)}, u32[]{:S(2)}) copy-start(s32[1024]{0:T(1024)S(1)} %iota.48) | copy-start | bytes 12292
  15.4 32.5 %copy-start.2 = (bf16[3,128,448]{1,2,0:T(8,128)(2,1)S(1)}, bf16[3,128,448]{1,2,0:T(8,128)(2,1)}, u32[]{:S(2)}) copy-start(bf16[3,128,448]{1,2,0:T(8,128)(2,1)} %param.19) | copy-start | bytes 1032196
  47.9 5.0 %slice-start = ((s32[1024]{0:T(1024)}), s32[512]{0:T(512)S(1)}, s32[]{:S(2)}) async-start(s32[1024]{0:T(1024)} %copy-done.4), calls=%async_computation.8 | async-start | bytes 4096 | tf_op jit(solution)/shard_map/slice | solution.py:26
  385.0 3.5 copy-start.1
  385.0 4.0 copy-start.6
  396.1 0.7 copy-start.5
  397.3 38.9 %all-to-all-start = ((s32[16,1,4]{2,1,0:T(1,128)}), s32[16,1,4]{2,1,0:T(1,128)S(1)}, u32[]{:S(2)}, u32[]{:S(2)}) async-start(s32[16,1,4]{2,1,0:T(1,128)} %broadcast_in_dim.104), calls=%async_computation.1 | async-start | bytes 16384 | tf_op jit(solution)/shard_map/all_to_all | solution.py:127
  436.2 36.5 %all-to-all-start.1 = ((bf16[16,4,14336]{2,1,0:T(4,128)(2,1)}), bf16[16,4,14336]{2,1,0:T(4,128)(2,1)}, u32[]{:S(2)}, u32[]{:S(2)}) async-start(bf16[16,4,14336]{2,1,0:T(4,128)(2,1)} %select_select_fusion), calls=%async_computation.2 | async-start | bytes 3670016 | tf_op jit(solution)/shard_map/all_to_all | solution.py:126
Sparse Core Ops, SparseCore 0:
  10.4 72.4 all-gather.8
  85.1 148.0 all-gather.4
  235.6 67.4 all-gather.10
  305.3 66.3 all-gather.6
  396.2 100.3 reduce-scatter.1
where the time goes:
time: 504 us; the launch traced here: 503 us
  waiting for transfers between devices  317 us (63%)
  matrix products  73.9 us (15%)
  local copies, waits for them, and re-layouts  41.3 us (8%)
  blocking collectives  28.2 us (6%)
  other arithmetic  17.1 us (3%)
  between operations  14.6 us (3%)
  starting transfers between devices  10.9 us (2%)
    all_gather x1, waiting for transfers between devices, body(): lax.all_gather(normalized_hidden, 'tensor', axis=0, tiled=True)  150 us
    all_gather x1, waiting for transfers between devices, body(): lax.all_gather(key_projection_weight, 'dp', axis=0, tiled=True)  54.5 us
    all_gather x1, waiting for transfers between devices, body(): lax.all_gather(value_projection_weight, 'dp', axis=0, tiled=True)  44.8 us
    dot_general x3, matrix products, body(): jnp.dot(stream_in, piece, preferred_element_type=jnp.float32)  39.9 us
    all_gather x1, blocking collectives, body(): lax.all_gather(adapter_update, 'tensor', axis=0, tiled=True)  28.2 us
    all_to_all x1, waiting for transfers between devices, body(): lax.all_to_all(taken, 'dp', split_axis=0, concat_axis=0, tiled=True)  28.2 us
    all_gather x1, waiting for transfers between devices, body(): lax.all_gather(query_projection_weight, 'dp', axis=0, tiled=True)  27.7 us
    gather x2, local copies, waits for them, and re-layouts, body(): taken = jnp.take(stacked, source_rows.reshape(-1), axis=0)  11.8 us
  transfers between devices with their start and end apart: 7, of which 6 were waited for; matrix products, arithmetic and copies ran while one was open for 21% of the time, Pallas kernels for 0%

commit v1 on v0

--- a/solution.py
+++ b/solution.py
@@ -1,3 +1,4 @@
+import functools
 import math
 import jax
 import jax.numpy as jnp
@@ -7,6 +8,19 @@
 HD = 224
 epsilon = 1e-05
 negative = -1e30
+
+
+def marks_pack(state, which_axis):
+    heard = jnp.concatenate(
+        jax.lax.all_to_all(
+            jnp.stack([state] * jax.lax.axis_size(which_axis), axis=0), which_axis, 0, 0
+        ),
+        axis=0,
+    )
+    return heard
+
+
+_supply_outputs = functools.partial(marks_pack, which_axis="tensor")
 
 
 def normalize(hidden_state_input, token_embedding_input, input_norm_gain):
@@ -59,7 +73,7 @@
         normalized_hidden, adapter_down_maps, preferred_element_type=jnp.float32
     ).astype(jnp.bfloat16)
     stream_in, stream_low = (
-        lax.all_gather(normalized_hidden, "tensor", axis=0, tiled=True),
+        _supply_outputs(normalized_hidden),
         lax.all_gather(adapter_update, "tensor", axis=0, tiled=True),
     )
     pieces = (

time: 504 us -> 451 us (0.89)
  waiting for transfers between devices: 317 us -> 37.5 us
  blocking collectives: 28.2 us -> 235 us
  starting transfers between devices: 10.9 us -> 25.7 us
  local copies, waits for them, and re-layouts: 41.3 us -> 47.8 us
    all_gather x1, blocking collectives: 28.2 us -> 235 us  [body(): lax.all_gather(adapter_update, 'tensor', axis=0, tiled=True)]
    all_gather x1 -> x0, waiting for transfers between devices: 150 us -> none  [body(): lax.all_gather(normalized_hidden, 'tensor', axis=0, tiled=True)]
    all_gather x1, waiting for transfers between devices: 54.5 us -> 0.01 us  [body(): lax.all_gather(key_projection_weight, 'dp', axis=0, tiled=True)]
    all_gather x1, waiting for transfers between devices: 44.8 us -> 0.01 us  [body(): lax.all_gather(value_projection_weight, 'dp', axis=0, tiled=True)]
    all_gather x1, waiting for transfers between devices: 27.7 us -> 0.01 us  [body(): lax.all_gather(query_projection_weight, 'dp', axis=0, tiled=True)]
    all_to_all x1, starting transfers between devices: 3.63 us -> 11.4 us  [body(): lax.all_to_all(row_send, 'dp', split_axis=0, concat_axis=0, tiled=True)]
    all_to_all x0 -> x1, starting transfers between devices: none -> 7 us  [marks_pack(): jax.lax.all_to_all(jnp.stack([state] * jax.lax.axis_size(which_axis), axi...]
    another operation x0 -> x1, local copies, waits for them, and re-layouts: none -> 5.42 us  [marks_pack(): jnp.stack([state] * jax.lax.axis_size(which_axis), axis=0)]
  transfers between devices with their start and end apart: 7 -> 7, of which waited for: 6 -> 2; matrix products, arithmetic and copies ran while one was open for 21% -> 25% of each run, Pallas kernels for 0% -> 0%
where the time goes in v1:
time: 451 us; the launch traced here: 450 us
  blocking collectives  235 us (52%)
  matrix products  74 us (16%)
  local copies, waits for them, and re-layouts  47.8 us (11%)
  waiting for transfers between devices  37.5 us (8%)
  starting transfers between devices  25.7 us (6%)
  other arithmetic  15.7 us (3%)
  between operations  14.6 us (3%)
    all_gather x1, blocking collectives, body(): lax.all_gather(adapter_update, 'tensor', axis=0, tiled=True)  235 us
    dot_general x3, matrix products, body(): jnp.dot(stream_in, piece, preferred_element_type=jnp.float32)  40.2 us
    all_to_all x1, waiting for transfers between devices, body(): lax.all_to_all(taken, 'dp', split_axis=0, concat_axis=0, tiled=True)  28.2 us
    gather x2, local copies, waits for them, and re-layouts, body(): taken = jnp.take(stacked, source_rows.reshape(-1), axis=0)  11.8 us
    all_to_all x1, starting transfers between devices, body(): lax.all_to_all(row_send, 'dp', split_axis=0, concat_axis=0, tiled=True)  11.4 us
    sub x2, matrix products, attend_block(): expo = jnp.exp(scores - top)  10.4 us
  transfers between devices with their start and end apart: 7, of which 2 were waited for; matrix products, arithmetic and copies ran while one was open for 25% of the time, Pallas kernels for 0%

profile of v1, /device:TPU:1, one launch (start us, length us, event | category | flops | bytes accessed | tf_op | source)
XLA Modules:
  0.0 450.3 jit_solution(7386189608324522089)
XLA Ops:
  8.7 1.9 fusion.2
  10.6 2.0 fusion.4
  13.8 5.4 %stack.8 = bf16[8,128,7168]{2,1,0:T(8,128)(2,1)} broadcast(bf16[128,7168]{1,0:T(8,128)(2,1)S(1)} %fusion.4), dimensions={1,2} | broadcast | bytes 16515072 | tf_op jit(solution)/shard_map/stack | solution.py:16
  19.2 7.0 %all-to-all-start = ((bf16[8,128,7168]{2,1,0:T(8,128)(2,1)}), bf16[8,128,7168]{2,1,0:T(8,128)(2,1)}, u32[]{:S(2)}, u32[]{:S(2)}) async-start(bf16[8,128,7168]{2,1,0:T(8,128)(2,1)} %stack.8), calls=%async_computation | async-start | bytes 29360128 | tf_op jit(solution)/shard_map/all_to_all | solution.py:15
  27.8 4.3 convolution_convert_fusion.2
  32.1 234.9 %all_gather.13 = bf16[1024,384]{1,0:T(8,128)(2,1)S(1)} all-gather(bf16[128,384]{1,0:T(8,128)(2,1)S(1)} %convolution_convert_fusion.2), channel_id=1, replica_groups=mesh['dp'=16,'tensor'=8] {'tensor'}, dimensions={0}, use_global_device_ids=true | all-gather | bytes 884736 | tf_op jit(solution)/shard_map/all_gather | solution.py:77
  267.0 1.6 fusion.26
  268.6 1.7 fusion.28
  270.3 1.6 fusion.30
  271.9 2.1 fusion.14
  274.1 13.3 %add_convert_fusion.1 = bf16[1024,448]{0,1:T(8,128)(2,1)} fusion(f32[1024,448]{0,1:T(8,128)} %fusion.28, bf16[1024,7168]{1,0:T(8,128)(2,1)} %bitcast.1, bf16[7168,448]{1,0:T(8,128)(2,1)} %all-gather.6.cloned.1.call-done), kind=kOutput, calls=%fused_computation.36 | convolution fusion | flops 6577586176 | bytes 23855104 | tf_op jit(solution)/shard_map/dot_general | solution.py:85
  287.4 2.1 fusion.49
  289.5 13.3 %add_convert_fusion = bf16[1024,448]{0,1:T(8,128)(2,1)} fusion(f32[1024,448]{0,1:T(8,128)} %fusion.26, bf16[1024,7168]{1,0:T(8,128)(2,1)} %bitcast.1, bf16[7168,448]{1,0:T(8,128)(2,1)} %all-gather.8.cloned.1.call-done), kind=kOutput, calls=%fused_computation.35 | convolution fusion | flops 6577586176 | bytes 23855104 | tf_op jit(solution)/shard_map/dot_general | solution.py:85
  302.9 5.2 %fusion.52 = (f32[2,512]{1,0:T(2,128)S(1)}, f32[2,512,1024]{2,1,0:T(8,128)}) fusion(pred[512,1024]{1,0:T(8,128)(4,1)} %get-tuple-element.6, bf16[512,2,224]{0,2,1:T(8,128)(2,1)} %bitcast.62, bf16[1024,2,224]{0,2,1:T(8,128)(2,1)} %bitcast.55), kind=kOutput, calls=%fused_computation.86 | convolution fusion | flops 473957376 | bytes 6098944 | tf_op jit(solution)/shard_map/sub | solution.py:48
  308.0 5.3 %fusion.51 = (f32[2,512]{1,0:T(2,128)S(1)}, f32[2,512,1024]{2,1,0:T(8,128)}) fusion(pred[512,1024]{1,0:T(8,128)(4,1)} %get-tuple-element.7, bf16[512,2,224]{0,2,1:T(8,128)(2,1)} %bitcast.61, bf16[1024,2,224]{0,2,1:T(8,128)(2,1)} %bitcast.56), kind=kOutput, calls=%fused_computation.85 | convolution fusion | flops 473957376 | bytes 6098944 | tf_op jit(solution)/shard_map/sub | solution.py:48
  313.3 13.5 %add_convert_fusion.2 = bf16[1024,448]{0,1:T(8,128)(2,1)} fusion(f32[1024,448]{0,1:T(8,128)} %fusion.30, bf16[1024,7168]{1,0:T(8,128)(2,1)} %bitcast.1, bf16[7168,448]{1,0:T(8,128)(2,1)} %all-gather.4.cloned.1.call-done), kind=kOutput, calls=%fused_computation.37 | convolution fusion | flops 6577586176 | bytes 23855104 | tf_op jit(solution)/shard_map/dot_general | solution.py:85
  326.8 3.5 fusion.22
  331.7 6.1 %convolution_convert_fusion.1 = bf16[1024,3584]{1,0:T(8,128)(2,1)} fusion(bf16[448,3584]{1,0:T(8,128)(2,1)S(1)} %copy-done, bf16[512,448]{0,1:T(8,128)(2,1)S(1)} %bitcast.66, bf16[512,448]{0,1:T(8,128)(2,1)S(1)} %bitcast.65), kind=kOutput, calls=%fused_computation.4 | convolution fusion | flops 3293839360 | bytes 11468800 | tf_op jit(solution)/shard_map/dot_general | solution.py:111
  339.1 11.4 %all-to-all-start.1 = ((s32[16,1,4]{2,1,0:T(1,128)}), s32[16,1,4]{2,1,0:T(1,128)S(1)}, u32[]{:S(2)}, u32[]{:S(2)}) async-start(s32[16,1,4]{2,1,0:T(1,128)} %broadcast_in_dim.104), calls=%async_computation.2 | async-start | bytes 16384 | tf_op jit(solution)/shard_map/all_to_all | solution.py:141
  352.4 3.9 broadcast_in_dim.106
  357.5 3.9 broadcast_in_dim.108
  361.5 2.9 pad_maximum_fusion.1
  364.4 3.9 copy.17
  368.3 7.5 %gather_fusion = bf16[1024,896]{1,0:T(8,128)(2,1)} fusion(bf16[1024,896]{1,0:T(8,128)(2,1)} %copy.17, s32[1024]{0:T(1024)S(1)} %broadcast_clamp_fusion), kind=kCustom, calls=%fused_computation | custom fusion | bytes 3674112 | tf_op jit(solution)/shard_map/jit(_take)/gather | solution.py:135
  375.7 4.4 gather.7
  380.1 5.5 %select_select_fusion = bf16[16,4,14336]{2,1,0:T(4,128)(2,1)} fusion(pred[16,4,14336]{2,1,0:T(4,128)(4,1)} %broadcast_in_dim.106, pred[16,4,14336]{2,1,0:T(4,128)(4,1)} %broadcast_in_dim.108, bf16[16,4,14336]{2,1,0:T(4,128)(2,1)} %gather.7), kind=kLoop, calls=%fused_computation.34 | loop fusion | flops 1835008 | bytes 5505024 | tf_op jit(solution)/shard_map/jit(_where)/select_n | solution.py:136
  385.6 7.2 %all-to-all-start.2 = ((bf16[16,4,14336]{2,1,0:T(4,128)(2,1)}), bf16[16,4,14336]{2,1,0:T(4,128)(2,1)}, u32[]{:S(2)}, u32[]{:S(2)}) async-start(bf16[16,4,14336]{2,1,0:T(4,128)(2,1)} %select_select_fusion), calls=%async_computation.3 | async-start | bytes 3670016 | tf_op jit(solution)/shard_map/all_to_all | solution.py:140
  394.1 28.2 %all-to-all-done.2 = bf16[16,4,14336]{2,1,0:T(4,128)(2,1)} async-done(((bf16[16,4,14336]{2,1,0:T(4,128)(2,1)}), bf16[16,4,14336]{2,1,0:T(4,128)(2,1)}, u32[]{:S(2)}, u32[]{:S(2)}) %all-to-all-start.2) | async-done | bytes 1835040 | tf_op jit(solution)/shard_map/all_to_all | solution.py:140
  422.2 3.9 reshape.334
  426.1 3.6 convolution_convert_fusion
  429.7 6.8 %reshape.335 = bf16[64,16,2,448]{3,2,1,0:T(2,128)(2,1)} reshape(bf16[64,14336]{1,0:T(8,128)(2,1)} %convolution_convert_fusion) | data formatting | bytes 3670016 | tf_op jit(solution)/shard_map/reshape | solution.py:151
  436.5 7.3 %reduce-scatter.2.cloned.1.call-done = bf16[128,3584]{1,0:T(8,128)(2,1)} async-done(((bf16[1024,3584]{1,0:T(8,128)(2,1)}), bf16[128,3584]{1,0:T(8,128)(2,1)}) %reduce-scatter.2.cloned.1.call-update) | async-done | bytes 917520 | tf_op jit(solution)/shard_map/reduce_scatter | solution.py:110
  (55 shorter events, 10.5 us)
Async XLA Ops:
  7.2 324.6 %copy-start = (bf16[448,3584]{1,0:T(8,128)(2,1)S(1)}, bf16[448,3584]{1,0:T(8,128)(2,1)}, u32[]{:S(2)}) copy-start(bf16[448,3584]{1,0:T(8,128)(2,1)} %param.20) | copy-start | bytes 9633796
  7.2 266.9 %all-gather.6.cloned.1.call-start = ((), (), s32[]{:S(2)}) async-start(), calls=%async_computation.5 | async-start | bytes 7798784 | tf_op jit(solution)/shard_map/all_gather | solution.py:80
  7.9 281.6 %all-gather.8.cloned.1.call-start = ((), (), s32[]{:S(2)}) async-start(), calls=%async_computation.6 | async-start | bytes 7798784 | tf_op jit(solution)/shard_map/all_gather | solution.py:81
  12.6 1.2 copy-start.1
  19.2 8.5 %copy-start.4 = (s32[1024]{0:T(1024)S(1)}, s32[1024]{0:T(1024)}, u32[]{:S(2)}) copy-start(s32[1024]{0:T(1024)} %param.21) | copy-start | bytes 12292
  19.2 254.9 %all-to-all-start = ((bf16[8,128,7168]{2,1,0:T(8,128)(2,1)}), bf16[8,128,7168]{2,1,0:T(8,128)(2,1)}, u32[]{:S(2)}, u32[]{:S(2)}) async-start(bf16[8,128,7168]{2,1,0:T(8,128)(2,1)} %stack.8), calls=%async_computation | async-start | bytes 29360128 | tf_op jit(solution)/shard_map/all_to_all | solution.py:15
  26.2 287.1 %all-gather.4.cloned.1.call-start = ((), (), s32[]{:S(2)}) async-start(), calls=%async_computation.4 | async-start | bytes 7798784 | tf_op jit(solution)/shard_map/all_gather | solution.py:82
  27.0 416.8 %reduce-scatter.2.cloned.1.call-start = ((), (), s32[]{:S(2)}) async-start(), calls=%async_computation.7 | async-start | bytes 8257536 | tf_op jit(solution)/shard_map/reduce_scatter | solution.py:110
  27.7 4.4 copy-start.5
  27.7 239.3 %copy-start.3 = (bf16[3,128,448]{1,2,0:T(8,128)(2,1)S(1)}, bf16[3,128,448]{1,2,0:T(8,128)(2,1)}, u32[]{:S(2)}) copy-start(bf16[3,128,448]{1,2,0:T(8,128)(2,1)} %param.19) | copy-start | bytes 1032196
  267.0 4.9 %slice-start = ((s32[1024]{0:T(1024)}), s32[512]{0:T(512)S(1)}, s32[]{:S(2)}) async-start(s32[1024]{0:T(1024)} %copy-done.5), calls=%async_computation.8 | async-start | bytes 4096 | tf_op jit(solution)/shard_map/slice | solution.py:40
  326.8 3.5 copy-start.2
  326.8 4.0 copy-start.7
  337.9 0.7 copy-start.6
  339.1 46.5 %all-to-all-start.1 = ((s32[16,1,4]{2,1,0:T(1,128)}), s32[16,1,4]{2,1,0:T(1,128)S(1)}, u32[]{:S(2)}, u32[]{:S(2)}) async-start(s32[16,1,4]{2,1,0:T(1,128)} %broadcast_in_dim.104), calls=%async_computation.2 | async-start | bytes 16384 | tf_op jit(solution)/shard_map/all_to_all | solution.py:141
  385.6 36.6 %all-to-all-start.2 = ((bf16[16,4,14336]{2,1,0:T(4,128)(2,1)}), bf16[16,4,14336]{2,1,0:T(4,128)(2,1)}, u32[]{:S(2)}, u32[]{:S(2)}) async-start(bf16[16,4,14336]{2,1,0:T(4,128)(2,1)} %select_select_fusion), calls=%async_computation.3 | async-start | bytes 3670016 | tf_op jit(solution)/shard_map/all_to_all | solution.py:140
Sparse Core Ops, SparseCore 0:
  10.4 92.6 all-gather.5
  105.4 89.2 all-gather.7
  197.2 79.7 all-gather.3
  338.0 105.6 reduce-scatter.1
